TPU v7x, 32 devices: a whole 2x2x4 slice. The times are simulated.
32 devices in a mesh: groups: 2 (over x), heads: 4 (over y, core), seq: 4 (over z).
Axes of the slice: x: 2, y: 2, z: 4, core: 2. Of those that a mesh axis runs over, the one named last changes fastest.
Arguments:
- lin_query: bfloat16 [4096, 4096], P(('groups', 'seq'), 'heads'), parts along dimension 0, may hold values from -6 to 6
- lin_key: bfloat16 [4096, 4096], P(('groups', 'seq'), 'heads'), parts along dimension 0, may hold values from -6 to 6
- lin_value: bfloat16 [4096, 4096], P(('groups', 'seq'), 'heads'), parts along dimension 0, may hold values from -6 to 6
- log_decay: float32 [4096, 32], P(('groups', 'seq'), 'heads'), parts along dimension 0, may hold values from -1 to 0
- stream: bfloat16 [4096, 6144], P(('groups', 'seq'), 'heads'), parts along dimension 0, may hold values from -400 to 400
- out_weight: bfloat16 [4096, 6144], P('heads', 'seq'), may hold values from -0.125 to 0.125
- norm_gain: bfloat16 [6144], P('heads'), may hold values from 0.5 to 1.5
- query_weight: bfloat16 [6144, 4096], P('seq', 'heads'), may hold values from -12 to 12
- kv_weight: bfloat16 [4, 6144, 256], P(None, 'seq'), may hold values from -1 to 1
Outputs:
- stream_next: bfloat16 [4096, 6144], P(('groups', 'seq'), 'heads'), parts along dimension 0
- attended: bfloat16 [4096, 4096], P(('groups', 'seq'), 'heads'), parts along dimension 0
There are 2 independent parts, one for each index of `groups`. A program takes and returns all parts, laid end to end along the dimension named above; an argument that names none is the same for every part. Nothing has to cross between parts.
All inputs are finite; a program needn't handle non-finite values.
Results may differ from a plain program's by a relative error of at most 0.019.
Values may be sent and summed in bfloat16 or wider, within the bound.
No kernel may reach another device: no remote copies, remote signals or barrier semaphores. Data moves between devices by JAX's collectives and lax.ppermute only.
A program may use at most 128 MiB of HBM per device.

v0:
```python
import jax
import jax.numpy as jnp
from jax import lax
from jax.sharding import PartitionSpec as P

D = 6144
QUERY_HEADS = 32
KVH = 4
DH = 128
BLOCK = 256


def from_behind(value, axis, steps):
    count = lax.axis_size(axis)
    leading, last = (max(0, -steps), min(count, count - steps))
    return lax.ppermute(value, axis, [(source, source + steps) for source in range(leading, last)])


def lightning_block(kv_state, block_inputs):
    query_blk, key_blk, value_blk, decay_blk = block_inputs
    block_len = query_blk.shape[0]
    local_cum = jnp.cumsum(decay_blk, axis=0)
    causal_mask = (jnp.arange(block_len)[:, None] >= jnp.arange(block_len)[None, :])[:, :, None]
    decay_diff = local_cum[:, None, :] - local_cum[None, :, :]
    decays = jnp.where(causal_mask, jnp.exp(jnp.where(causal_mask, decay_diff, 0.0)), 0.0)
    scores = jnp.einsum("thd,shd->hts", query_blk, key_blk, preferred_element_type=jnp.float32)
    weights = (scores * jnp.transpose(decays, (2, 0, 1))).astype(jnp.bfloat16)
    intra_out = jnp.einsum("hts,shd->thd", weights, value_blk, preferred_element_type=jnp.float32)
    query_f = query_blk.astype(jnp.float32)
    inter_out = jnp.einsum(
        "thd,hde->the",
        query_f * jnp.exp(local_cum)[:, :, None],
        kv_state,
        precision=lax.Precision.HIGHEST,
    )
    tail_decay = jnp.exp(local_cum[-1][None, :] - local_cum)
    key_f = key_blk.astype(jnp.float32) * tail_decay[:, :, None]
    kv_state = jnp.exp(local_cum[-1])[:, None, None] * kv_state + jnp.einsum(
        "shd,she->hde", key_f, value_blk.astype(jnp.float32), precision=lax.Precision.HIGHEST
    )
    return (kv_state, intra_out + inter_out)


def shards_base(
    lin_query, lin_key, lin_value, log_decay, stream, out_weight, norm_gain, query_weight, kv_weight
):
    tok_rows = lin_query.shape[0]
    heads_here = log_decay.shape[1]
    head_width = heads_here * DH
    nblocks = tok_rows // BLOCK
    block_shape = (nblocks, BLOCK, heads_here, DH)
    inputs = (
        lin_query.reshape(block_shape),
        lin_key.reshape(block_shape),
        lin_value.reshape(block_shape),
        log_decay.reshape(nblocks, BLOCK, heads_here),
    )
    start_state = jnp.zeros((heads_here, DH, DH), jnp.float32)
    local_state, local_out = lax.scan(lightning_block, start_state, inputs)
    local_out = local_out.reshape(tok_rows, heads_here, DH)
    decay_total = jnp.sum(log_decay, axis=0)
    totals, states = (
        lax.all_gather(decay_total[None].astype(jnp.bfloat16), "seq", axis=0, tiled=True).astype(
            jnp.float32
        ),
        lax.all_gather(local_state[None].astype(jnp.bfloat16), "seq", axis=0, tiled=True).astype(
            jnp.float32
        ),
    )
    position = lax.axis_index("seq")
    device_order = jnp.arange(totals.shape[0])
    earlier = (device_order < position)[:, None]
    before = jnp.sum(jnp.where(earlier, totals, 0.0), axis=0)
    inclusive = jnp.cumsum(totals, axis=0)
    factors = jnp.where(earlier, jnp.exp(jnp.where(earlier, before[None, :] - inclusive, 0.0)), 0.0)
    incoming = jnp.einsum("jh,jhde->hde", factors, states, precision=lax.Precision.HIGHEST)
    running = jnp.cumsum(log_decay, axis=0)
    query_f = (
        lin_query.reshape(tok_rows, heads_here, DH).astype(jnp.float32)
        * jnp.exp(running)[:, :, None]
    )
    carried = jnp.einsum("thd,hde->the", query_f, incoming, precision=lax.Precision.HIGHEST)
    lin_raw = local_out + carried
    lin_out = (
        (lin_raw * lax.rsqrt(jnp.mean(lin_raw * lin_raw, axis=-1, keepdims=True) + 1e-06))
        .astype(jnp.bfloat16)
        .reshape(tok_rows, head_width)
    )
    branch = jnp.dot(
        lin_out,
        lax.all_gather(out_weight, "seq", axis=1, tiled=True),
        preferred_element_type=jnp.float32,
    )
    kv_group = lax.axis_index("heads") * heads_here // (QUERY_HEADS // KVH)
    kv_mine = lax.dynamic_index_in_dim(kv_weight, kv_group, 0, keepdims=False)
    query_rows, kv_rows = (
        lax.all_gather(query_weight, "seq", axis=0, tiled=True),
        lax.all_gather(kv_mine, "seq", axis=0, tiled=True),
    )
    projection = jnp.concatenate([query_rows, kv_rows], axis=1)
    own_sum = lax.psum_scatter(
        branch.astype(jnp.bfloat16), "heads", scatter_dimension=1, tiled=True
    ).astype(jnp.float32)
    mixed_sum = stream.astype(jnp.float32) + own_sum
    stream_next = mixed_sum.astype(jnp.bfloat16)
    total_sq = lax.psum(jnp.sum(mixed_sum * mixed_sum, axis=1), "heads")
    normed = (
        mixed_sum
        * lax.rsqrt(total_sq / D + 1e-05)[:, None]
        * norm_gain.astype(jnp.float32)[None, :]
    ).astype(jnp.bfloat16)
    projected = jnp.dot(
        lax.all_gather(normed, "heads", axis=1, tiled=True),
        projection,
        preferred_element_type=jnp.float32,
    )
    projected = projected.astype(jnp.bfloat16)
    queries = projected[:, :head_width].reshape(tok_rows, heads_here, DH)
    keys_values = projected[:, head_width:]
    position = lax.axis_index("seq")
    query_pos = position * tok_rows + jnp.arange(tok_rows)
    score_scale = float(DH) ** (-0.5)

    def attend(state_in, kv_block, key_start):
        old_max, row_total, weighted = state_in
        key_count = kv_block.shape[0]
        key_part = kv_block[:, :DH]
        value_part = kv_block[:, DH:]
        scores = (
            jnp.einsum("thd,sd->hts", queries, key_part, preferred_element_type=jnp.float32)
            * score_scale
        )
        key_pos = key_start + jnp.arange(key_count)
        allowed = ((key_pos[None, :] <= query_pos[:, None]) & (key_pos[None, :] >= 0))[None, :, :]
        scores = jnp.where(allowed, scores, -1e30)
        new_max = jnp.maximum(old_max, jnp.max(scores, axis=-1))
        expos = jnp.where(allowed, jnp.exp(scores - new_max[:, :, None]), 0.0)
        rescale = jnp.exp(old_max - new_max)
        row_total = row_total * rescale + jnp.sum(expos, axis=-1)
        prob_bf16 = expos.astype(jnp.bfloat16)
        weighted = weighted * rescale[:, :, None] + jnp.einsum(
            "hts,sd->htd", prob_bf16, value_part, preferred_element_type=jnp.float32
        )
        return (new_max, row_total, weighted)

    initial = (
        jnp.full((heads_here, tok_rows), -1e30, jnp.float32),
        jnp.zeros((heads_here, tok_rows), jnp.float32),
        jnp.zeros((heads_here, tok_rows, DH), jnp.float32),
    )
    first_state = attend(initial, keys_values, position * tok_rows)
    seq_count = lax.axis_size("seq")

    def cycle_turn(turn_index, loop_state):
        moving, inner_state = loop_state
        moving = from_behind(moving, "seq", 1)
        source = position - turn_index
        return (moving, attend(inner_state, moving, source * tok_rows))

    _, final_state = lax.fori_loop(1, seq_count, cycle_turn, (keys_values, first_state))
    _, row_total, weighted = final_state
    attended = (
        jnp.transpose(weighted / row_total[:, :, None], (1, 0, 2))
        .reshape(tok_rows, head_width)
        .astype(jnp.bfloat16)
    )
    return (stream_next, attended)


def lightning_local(lin_query, lin_key, lin_value, log_decay):
    tok_rows = lin_query.shape[0]
    heads_here = log_decay.shape[1]
    nblocks = tok_rows // BLOCK
    shape4 = (tok_rows, heads_here, DH)
    q4, k4, v4 = (x.reshape(shape4) for x in (lin_query, lin_key, lin_value))
    state = jnp.zeros((heads_here, DH, DH), jnp.float32)
    outs = []
    for blk in range(nblocks):
        rows = slice(blk * BLOCK, (blk + 1) * BLOCK)
        state, out = lightning_block(state, (q4[rows], k4[rows], v4[rows], log_decay[rows]))
        outs.append(out)
    local_out = jnp.concatenate(outs, axis=0)
    decay_total = jnp.sum(log_decay, axis=0)
    packed = jnp.concatenate([state.reshape(-1), decay_total]).astype(jnp.bfloat16)
    gathered = lax.all_gather(packed, "seq", axis=0, tiled=False).astype(jnp.float32)
    state_size = state.size
    states = gathered[:, :state_size].reshape((-1,) + state.shape)
    totals = gathered[:, state_size:]
    position = lax.axis_index("seq")
    device_order = jnp.arange(totals.shape[0])
    earlier = (device_order < position)[:, None]
    before = jnp.sum(jnp.where(earlier, totals, 0.0), axis=0)
    inclusive = jnp.cumsum(totals, axis=0)
    factors = jnp.where(earlier, jnp.exp(jnp.where(earlier, before[None, :] - inclusive, 0.0)), 0.0)
    incoming = jnp.einsum("jh,jhde->hde", factors, states, precision=lax.Precision.HIGHEST)
    running = jnp.cumsum(log_decay, axis=0)
    query_f = q4.astype(jnp.float32) * jnp.exp(running)[:, :, None]
    carried = jnp.einsum("thd,hde->the", query_f, incoming, precision=lax.Precision.HIGHEST)
    lin_raw = local_out + carried
    lin_out = (
        (lin_raw * lax.rsqrt(jnp.mean(lin_raw * lin_raw, axis=-1, keepdims=True) + 1e-06))
        .astype(jnp.bfloat16)
        .reshape(tok_rows, heads_here * DH)
    )
    return lin_out


def attend_block(queries, query_pos, state_in, kv_block, key_start):
    old_max, row_total, weighted = state_in
    key_count = kv_block.shape[0]
    key_part = kv_block[:, :DH]
    value_part = kv_block[:, DH:]
    score_scale = float(DH) ** (-0.5)
    scores = (
        jnp.einsum("thd,sd->hts", queries, key_part, preferred_element_type=jnp.float32)
        * score_scale
    )
    key_pos = key_start + jnp.arange(key_count)
    allowed = ((key_pos[None, :] <= query_pos[:, None]) & (key_pos[None, :] >= 0))[None, :, :]
    scores = jnp.where(allowed, scores, -1e30)
    new_max = jnp.maximum(old_max, jnp.max(scores, axis=-1))
    expos = jnp.where(allowed, jnp.exp(scores - new_max[:, :, None]), 0.0)
    rescale = jnp.exp(old_max - new_max)
    row_total = row_total * rescale + jnp.sum(expos, axis=-1)
    prob_bf16 = expos.astype(jnp.bfloat16)
    weighted = weighted * rescale[:, :, None] + jnp.einsum(
        "hts,sd->htd", prob_bf16, value_part, preferred_element_type=jnp.float32
    )
    return (new_max, row_total, weighted)


def shards_fast(
    lin_query, lin_key, lin_value, log_decay, stream, out_weight, norm_gain, query_weight, kv_weight
):
    n_heads = lax.axis_size("heads")
    n_seq = lax.axis_size("seq")
    tok_rows = lin_query.shape[0]
    heads_here = log_decay.shape[1]
    head_width = heads_here * DH
    mine_a = lax.axis_index("heads")
    mine_b = lax.axis_index("seq")
    swap = [(x * n_seq + y, y * n_seq + x) for x in range(n_heads) for y in range(n_seq)]
    stream_t = lax.ppermute(stream, ("heads", "seq"), swap)
    lin_out = lightning_local(lin_query, lin_key, lin_value, log_decay)
    lin_all = lax.all_gather(lin_out, "seq", axis=0, tiled=True)
    part = jnp.dot(lin_all, out_weight, preferred_element_type=jnp.float32).astype(jnp.bfloat16)
    own_sum = lax.psum_scatter(part, "heads", scatter_dimension=0, tiled=True)
    mixed_sum = stream_t.astype(jnp.float32) + own_sum.astype(jnp.float32)
    stream_next = lax.ppermute(mixed_sum.astype(jnp.bfloat16), ("heads", "seq"), swap)
    total_sq = lax.psum(jnp.sum(mixed_sum * mixed_sum, axis=1), "seq")
    cols = mixed_sum.shape[1]
    gain_all = lax.all_gather(norm_gain, "heads", axis=0, tiled=True)
    gain_b = lax.dynamic_slice_in_dim(gain_all, mine_b * cols, cols)
    normed = (
        mixed_sum * lax.rsqrt(total_sq / D + 1e-05)[:, None] * gain_b.astype(jnp.float32)[None, :]
    ).astype(jnp.bfloat16)
    normed_all = lax.all_gather(normed, "heads", axis=0, tiled=True)
    kv_group = mine_a * heads_here // (QUERY_HEADS // KVH)
    kv_mine = lax.dynamic_index_in_dim(kv_weight, kv_group, 0, keepdims=False)
    projection = jnp.concatenate([query_weight, kv_mine], axis=1)
    part2 = jnp.dot(normed_all, projection, preferred_element_type=jnp.float32).astype(jnp.bfloat16)
    reduced = lax.psum_scatter(part2, "seq", scatter_dimension=0, tiled=True)
    queries = reduced[:, :head_width].reshape(tok_rows, heads_here, DH)
    kv_own = reduced[:, head_width:]
    query_pos = mine_b * tok_rows + jnp.arange(tok_rows)
    state = (
        jnp.full((heads_here, tok_rows), -1e30, jnp.float32),
        jnp.zeros((heads_here, tok_rows), jnp.float32),
        jnp.zeros((heads_here, tok_rows, DH), jnp.float32),
    )
    earlier_kv = [from_behind(kv_own, "seq", dist) for dist in range(1, n_seq)]
    state = attend_block(queries, query_pos, state, kv_own, mine_b * tok_rows)
    for dist in range(1, n_seq):
        key_start = (mine_b - dist) * tok_rows
        state = attend_block(queries, query_pos, state, earlier_kv[dist - 1], key_start)
    _, row_total, weighted = state
    attended = (
        jnp.transpose(weighted / row_total[:, :, None], (1, 0, 2))
        .reshape(tok_rows, head_width)
        .astype(jnp.bfloat16)
    )
    return (stream_next, attended)


def solution(mesh):
    n_heads = mesh.shape["heads"]
    n_seq = mesh.shape["seq"]
    fast_ok = n_heads == n_seq and QUERY_HEADS % n_heads == 0
    if fast_ok:
        heads_here = QUERY_HEADS // n_heads
        fast_ok = QUERY_HEADS // KVH % heads_here == 0 and D % n_seq == 0
    shards = shards_fast if fast_ok else shards_base
    return jax.shard_map(
        shards,
        mesh=mesh,
        in_specs=(
            P(("groups", "seq"), "heads"),
            P(("groups", "seq"), "heads"),
            P(("groups", "seq"), "heads"),
            P(("groups", "seq"), "heads"),
            P(("groups", "seq"), "heads"),
            P("heads", "seq"),
            P("heads"),
            P("seq", "heads"),
            P(None, "seq", None),
        ),
        out_specs=(P(("groups", "seq"), "heads"), P(("groups", "seq"), "heads")),
        check_vma=False,
    )
```

profile of v0, /device:TPU:28, one launch (start us, length us, event | category | flops | bytes accessed | tf_op | source)
XLA Modules:
  0.0 567.0 jit_solution(838677574151914979)
XLA Ops:
  7.2 0.9 slice_bitcast_fusion.19
  10.3 0.9 reduce_sum.80
  11.2 2.2 fusion.108
  13.4 2.1 copy.237
  15.5 2.2 fusion.109
  17.7 2.0 copy.238
  19.8 2.0 copy.239
  21.8 2.0 copy.240
  23.8 1.9 convolution_add_fusion.1
  26.5 1.9 fusion.43
  28.4 0.9 concatenate.22
  29.3 3.3 maximum_bitcast_fusion
  33.2 2.2 fusion.107
  35.4 1.1 reduce-window.26
  36.7 2.1 copy.242
  38.8 2.0 copy.241
  41.0 3.4 fusion.38
  44.4 4.3 fusion.42
  48.7 3.3 fusion.40
  52.0 4.5 fusion.41
  56.5 20.7 %all-gather.10.cloned.1.call-done = bf16[4,1,131080]{2,1,0:T(2,128)(2,1)} async-done(((bf16[1,1,131080]{2,1,0:T(2,128)(2,1)}), bf16[4,1,131080]{2,1,0:T(2,128)(2,1)}) %all-gather.10.cloned.1.call-update) | async-done | bytes 1048656 | tf_op jit(solution)/shard_map/all_gather | solution.py:185
  77.2 2.6 copy.280
  79.9 1.3 slice_bitcast_fusion.1
  81.3 1.5 copy.246
  83.5 2.7 multiply_reduce_fusion.2
  86.2 1.5 multiply_convert_fusion.1
  87.7 2.3 copy.188
  90.0 11.4 %reduce-scatter.3.cloned.1.call-start = ((), (), s32[]{:S(2)}) async-start(), calls=%async_computation.3 | async-start | bytes 7864320 | tf_op jit(solution)/shard_map/reduce_scatter | solution.py:247
  101.4 67.9 %all-gather.6.cloned.1.call-done = bf16[2048,1024]{0,1:T(8,128)(2,1)} async-done(((bf16[512,1024]{0,1:T(8,128)(2,1)}), bf16[2048,1024]{0,1:T(8,128)(2,1)}) %all-gather.6.cloned.1.call-update) | async-done | bytes 4194320 | tf_op jit(solution)/shard_map/all_gather | solution.py:245
  169.3 11.0 %convolution_convert_fusion.1 = bf16[2048,1536]{1,0:T(8,128)(2,1)} fusion(bf16[2048,1024]{0,1:T(8,128)(2,1)} %all-gather.6.cloned.1.call-done, bf16[1024,1536]{1,0:T(8,128)(2,1)S(1)} %copy-done), kind=kOutput, calls=%fused_computation.9 | convolution fusion | flops 6445596672 | bytes 13631488 | tf_op jit(solution)/shard_map/dot_general | solution.py:246
  180.4 2.8 collective-permute-start
  183.2 6.2 %all-gather.1 = bf16[4,1,1536]{2,1,0:T(2,128)(2,1)S(1)} all-gather(bf16[1,1,1536]{2,1,0:T(2,128)(2,1)S(1)} %reshape.428), channel_id=1, replica_groups=mesh['groups'=2,'heads'=4,'seq'=4] {'heads'}, dimensions={0}, use_global_device_ids=true | all-gather | bytes 15360 | tf_op jit(solution)/shard_map/all_gather | solution.py:252
  189.6 30.6 %collective-permute-done = bf16[512,1536]{1,0:T(8,128)(2,1)S(1)} collective-permute-done((bf16[512,1536]{1,0:T(8,128)(2,1)}, bf16[512,1536]{1,0:T(8,128)(2,1)S(1)}, u32[]{:S(2)}, u32[]{:S(2)}) %collective-permute-start) | collective-permute-done | bytes 1572896 | tf_op jit(solution)/shard_map/ppermute | solution.py:243
  220.2 40.5 %reduce-scatter.3.cloned.1.call-done = bf16[512,1536]{1,0:T(8,128)(2,1)} async-done(((bf16[2048,1536]{1,0:T(8,128)(2,1)}), bf16[512,1536]{1,0:T(8,128)(2,1)}) %reduce-scatter.3.cloned.1.call-update) | async-done | bytes 1572880 | tf_op jit(solution)/shard_map/reduce_scatter | solution.py:247
  260.7 2.1 multiply_reduce_fusion
  262.8 12.8 %psum.7 = f32[512]{0:T(512)S(1)} all-reduce(f32[512]{0:T(512)S(1)} %multiply_reduce_fusion), channel_id=1, replica_groups=mesh['groups'=2,'heads'=4,'seq'=4] {'seq'}, use_global_device_ids=true, to_apply=%region_12.13 | all-reduce | flops 512 | bytes 4096 | tf_op jit(solution)/shard_map/psum | solution.py:250
  275.6 2.3 multiply_convert_fusion
  278.0 1.2 dynamic-slice_bitcast_fusion
  279.1 45.4 %all-gather.8.cloned.1.call-done = bf16[2048,1536]{1,0:T(8,128)(2,1)} async-done(((bf16[512,1536]{1,0:T(8,128)(2,1)}), bf16[2048,1536]{1,0:T(8,128)(2,1)}) %all-gather.8.cloned.1.call-update) | async-done | bytes 6291472 | tf_op jit(solution)/shard_map/all_gather | solution.py:257
  324.5 12.9 %convolution_convert_fusion = bf16[2048,1280]{1,0:T(8,128)(2,1)} fusion(bf16[2048,1536]{1,0:T(8,128)(2,1)} %all-gather.8.cloned.1.call-done, bf16[1536,256]{1,0:T(8,128)(2,1)S(1)} %dynamic-slice_bitcast_fusion, bf16[1536,1024]{1,0:T(8,128)(2,1)} %param.16), kind=kOutput, calls=%fused_computation.8 | convolution fusion | flops 8063549440 | bytes 15466496 | tf_op jit(solution)/shard_map/dot_general | solution.py:261
  337.4 1.4 copy-done.8
  338.8 2.3 collective-permute-start.1
  341.2 1.7 compare_and_fusion.3
  342.9 101.0 %collective-permute-done.1 = bf16[512,1536]{1,0:T(8,128)(2,1)S(1)} collective-permute-done((bf16[512,1536]{1,0:T(8,128)(2,1)S(1)}, bf16[512,1536]{1,0:T(8,128)(2,1)S(1)}, u32[]{:S(2)}, u32[]{:S(2)}) %collective-permute-start.1) | collective-permute-done | bytes 1572896 | tf_op jit(solution)/shard_map/ppermute | solution.py:249
  443.9 41.8 %reduce-scatter.5.cloned.1.call-done = bf16[512,1280]{1,0:T(8,128)(2,1)} async-done(((bf16[2048,1280]{1,0:T(8,128)(2,1)}), bf16[512,1280]{1,0:T(8,128)(2,1)}) %reduce-scatter.5.cloned.1.call-update) | async-done | bytes 1310736 | tf_op jit(solution)/shard_map/reduce_scatter | solution.py:262
  485.7 1.0 slice.154
  486.6 1.3 collective-permute-start.2
  487.9 1.3 collective-permute-start.4
  489.2 1.3 collective-permute-start.3
  490.6 3.0 fusion
  493.6 15.3 %collective-permute-done.2 = bf16[512,256]{1,0:T(8,128)(2,1)S(1)} collective-permute-done((bf16[512,256]{1,0:T(8,128)(2,1)S(1)}, bf16[512,256]{1,0:T(8,128)(2,1)S(1)}, u32[]{:S(2)}, u32[]{:S(2)}) %collective-permute-start.2) | collective-permute-done | bytes 262176 | tf_op jit(solution)/shard_map/ppermute | solution.py:16
  508.9 1.5 fusion.1
  510.4 4.6 collective-permute-done.4
  515.0 1.6 fusion.3
  516.6 9.7 %collective-permute-done.3 = bf16[512,256]{1,0:T(8,128)(2,1)S(1)} collective-permute-done((bf16[512,256]{1,0:T(8,128)(2,1)S(1)}, bf16[512,256]{1,0:T(8,128)(2,1)S(1)}, u32[]{:S(2)}, u32[]{:S(2)}) %collective-permute-start.3) | collective-permute-done | bytes 262176 | tf_op jit(solution)/shard_map/ppermute | solution.py:16
  526.2 4.8 fusion.2
  531.0 4.2 fusion.4
  535.2 6.3 %fusion.8 = (f32[8,512]{1,0:T(8,128)S(1)}, f32[8,512]{1,0:T(8,128)S(1)}) fusion(f32[512,512,8]{1,0,2:T(8,128)} %get-tuple-element.46, f32[8,512]{1,0:T(8,128)S(1)} %get-tuple-element.18, pred[512,512]{0,1:T(8,128)(4,1)S(1)} %copy-done.9, f32[8,512]{1,0:T(8,128)S(1)} %get-tuple-element.17, f32[512,512,8]{1,0,2:T(8,128)S(1)} %get-tuple-element.44, ...), kind=kLoop, calls=%fused_computation.18 | loop fusion | flops 20963328 | bytes 17367040 | tf_op jit(solution)/shard_map/reduce_sum | solution.py:224
  541.6 2.2 fusion.18
  543.8 2.2 fusion.16
  545.9 5.6 fusion.14
  551.5 3.8 fusion.31
  555.3 2.3 copy.201
  557.6 2.7 copy.282
  (83 shorter events, 5.2 us)
Async XLA Ops:
  7.2 162.2 %copy-start = (bf16[1024,1536]{1,0:T(8,128)(2,1)S(1)}, bf16[1024,1536]{1,0:T(8,128)(2,1)}, u32[]{:S(2)}) copy-start(bf16[1024,1536]{1,0:T(8,128)(2,1)} %param.14) | copy-start | bytes 9437188
  7.2 70.1 %all-gather.10.cloned.1.call-start = ((), (), s32[]{:S(2)}) async-start(), calls=%async_computation.6 | async-start | bytes 2624000 | tf_op jit(solution)/shard_map/all_gather | solution.py:185
  23.8 11.6 %copy-start.12 = (f32[512,8]{0,1:T(8,128)S(1)}, f32[512,8]{0,1:T(8,128)}, u32[]{:S(2)}) copy-start(f32[512,8]{0,1:T(8,128)} %param.12) | copy-start | bytes 49156
  25.7 0.8 copy-start.3
  32.6 136.7 %all-gather.6.cloned.1.call-start = ((), (), s32[]{:S(2)}) async-start(), calls=%async_computation.2 | async-start | bytes 5242880 | tf_op jit(solution)/shard_map/all_gather | solution.py:245
  81.3 1.9 copy-start.4
  81.3 1.9 copy-start.5
  81.3 2.2 copy-start.6
  90.0 170.7 %reduce-scatter.3.cloned.1.call-start = ((), (), s32[]{:S(2)}) async-start(), calls=%async_computation.3 | async-start | bytes 7864320 | tf_op jit(solution)/shard_map/reduce_scatter | solution.py:247
  180.3 2.8 copy-start.14
  180.3 144.2 %all-gather.8.cloned.1.call-start = ((), (), s32[]{:S(2)}) async-start(), calls=%async_computation.4 | async-start | bytes 7864320 | tf_op jit(solution)/shard_map/all_gather | solution.py:257
  180.4 39.8 %collective-permute-start = (bf16[512,1536]{1,0:T(8,128)(2,1)}, bf16[512,1536]{1,0:T(8,128)(2,1)S(1)}, u32[]{:S(2)}, u32[]{:S(2)}) collective-permute-start(bf16[512,1536]{1,0:T(8,128)(2,1)} %param.13), channel_id=1, source_target_pairs={{0,0},{1,4},{2,8},{3,12},{4,1},{5,5},{6,9},{7,13},{8,2},{9,6},{10,... | collective-permute-start | bytes 4718600 | tf_op jit(solution)/shard_map/ppermute | solution.py:243
  260.7 14.9 %copy-start.2 = (bf16[512,1536]{1,0:T(8,128)(2,1)S(1)}, bf16[512,1536]{1,0:T(8,128)(2,1)}, u32[]{:S(2)}) copy-start(bf16[512,1536]{1,0:T(8,128)(2,1)} %reduce-scatter.3.cloned.1.call-done) | copy-start | bytes 4718596
  277.9 207.8 %reduce-scatter.5.cloned.1.call-start = ((), (), s32[]{:S(2)}) async-start(), calls=%async_computation.5 | async-start | bytes 6553600 | tf_op jit(solution)/shard_map/reduce_scatter | solution.py:262
  337.4 1.4 copy-start.8
  338.8 105.1 %collective-permute-start.1 = (bf16[512,1536]{1,0:T(8,128)(2,1)S(1)}, bf16[512,1536]{1,0:T(8,128)(2,1)S(1)}, u32[]{:S(2)}, u32[]{:S(2)}) collective-permute-start(bf16[512,1536]{1,0:T(8,128)(2,1)S(1)} %copy-done.8), channel_id=1, source_target_pairs={{0,0},{1,4},{2,8},{3,12},{4,1},{5,5},{6,9},{7,13},{8,2},{9,6},{10,... | collective-permute-start | bytes 4718600 | tf_op jit(solution)/shard_map/ppermute | solution.py:249
  443.9 49.7 %copy-start.7 = (bf16[512,1536]{1,0:T(8,128)(2,1)}, bf16[512,1536]{1,0:T(8,128)(2,1)S(1)}, u32[]{:S(2)}) copy-start(bf16[512,1536]{1,0:T(8,128)(2,1)S(1)} %collective-permute-done.1) | copy-start | bytes 4718596
  486.6 22.2 %collective-permute-start.2 = (bf16[512,256]{1,0:T(8,128)(2,1)S(1)}, bf16[512,256]{1,0:T(8,128)(2,1)S(1)}, u32[]{:S(2)}, u32[]{:S(2)}) collective-permute-start(bf16[512,256]{1,0:T(8,128)(2,1)S(1)} %slice.154), channel_id=1, source_target_pairs={{0,1},{1,2},{2,3},{4,5},{5,6},{6,7},{8,9},{9,10},{10,11},{12,13},{... | collective-permute-start | bytes 786440 | tf_op jit(solution)/shard_map/ppermute | solution.py:16
  487.9 27.0 %collective-permute-start.4 = (bf16[512,256]{1,0:T(8,128)(2,1)S(1)}, bf16[512,256]{1,0:T(8,128)(2,1)S(1)}, u32[]{:S(2)}, u32[]{:S(2)}) collective-permute-start(bf16[512,256]{1,0:T(8,128)(2,1)S(1)} %slice.154), channel_id=1, source_target_pairs={{0,3},{4,7},{8,11},{12,15},{16,19},{20,23},{24,27},{28,31}} | collective-permute-start | bytes 786440 | tf_op jit(solution)/shard_map/ppermute | solution.py:16
  489.2 37.0 %collective-permute-start.3 = (bf16[512,256]{1,0:T(8,128)(2,1)S(1)}, bf16[512,256]{1,0:T(8,128)(2,1)S(1)}, u32[]{:S(2)}, u32[]{:S(2)}) collective-permute-start(bf16[512,256]{1,0:T(8,128)(2,1)S(1)} %slice.154), channel_id=1, source_target_pairs={{0,2},{1,3},{4,6},{5,7},{8,10},{9,11},{12,14},{13,15},{16,18},{17,... | collective-permute-start | bytes 786440 | tf_op jit(solution)/shard_map/ppermute | solution.py:16
  490.5 18.3 %copy-start.10 = (pred[512,512]{0,1:T(8,128)(4,1)S(1)}, pred[512,512]{0,1:T(8,128)(4,1)}, u32[]{:S(2)}) copy-start(pred[512,512]{0,1:T(8,128)(4,1)} %get-tuple-element.40) | copy-start | bytes 786436
  490.6 18.3 %copy-start.13 = (bf16[512,1280]{1,0:T(8,128)(2,1)S(1)}, bf16[512,1280]{1,0:T(8,128)(2,1)}, u32[]{:S(2)}) copy-start(bf16[512,1280]{1,0:T(8,128)(2,1)} %reduce-scatter.5.cloned.1.call-done) | copy-start | bytes 3932164
  515.0 11.2 %copy-start.9 = (pred[512,512]{0,1:T(8,128)(4,1)S(1)}, pred[512,512]{0,1:T(8,128)(4,1)}, u32[]{:S(2)}) copy-start(pred[512,512]{0,1:T(8,128)(4,1)} %get-tuple-element.39) | copy-start | bytes 786436
  526.2 4.8 copy-start.11
  551.5 8.7 %copy-start.1 = (bf16[1024,1536]{1,0:T(8,128)(2,1)S(1)}, bf16[1024,1536]{1,0:T(8,128)(2,1)}, u32[]{:S(2)}) copy-start(bf16[1024,1536]{1,0:T(8,128)(2,1)} %param.14) | copy-start | bytes 9437188
Sparse Core Ops, SparseCore 0:
  32.7 44.4 all-gather.9
  90.1 79.1 all-gather.5
  180.5 80.1 reduce-scatter.2
  278.0 46.4 all-gather.7
  337.5 148.1 reduce-scatter.4
where the time goes:
time: 571 us; the launch traced here: 567 us
  waiting for transfers between devices  378 us (66%)
  matrix products  70.3 us (12%)
  local copies, waits for them, and re-layouts  38.9 us (7%)
  other arithmetic  26 us (5%)
  starting transfers between devices  20.9 us (4%)
  blocking collectives  19 us (3%)
  between operations  14.4 us (3%)
    ppermute x1, waiting for transfers between devices, shards_fast(): lax.ppermute(mixed_sum.astype(jnp.bfloat16), ('heads', 'seq'), swap)  101 us
    all_gather x1, waiting for transfers between devices, shards_fast(): lin_all = lax.all_gather(lin_out, 'seq', axis=0, tiled=True)  67.9 us
    all_gather x1, waiting for transfers between devices, shards_fast(): normed_all = lax.all_gather(normed, 'heads', axis=0, tiled=True)  45.4 us
    reduce_scatter x1, waiting for transfers between devices, shards_fast(): reduced = lax.psum_scatter(part2, 'seq', scatter_dimension=0, tiled=True)  41.8 us
    reduce_scatter x1, waiting for transfers between devices, shards_fast(): own_sum = lax.psum_scatter(part, 'heads', scatter_dimension=0, tiled=True)  40.5 us
    ppermute x1, waiting for transfers between devices, shards_fast(): stream_t = lax.ppermute(stream, ('heads', 'seq'), swap)  30.6 us
    ppermute x3, waiting for transfers between devices, from_behind(): lax.ppermute(value, axis, [(source, source + steps) for source in range(l...  29.5 us
    unnamed x43, local copies, waits for them, and re-layouts  25.2 us
  transfers between devices with their start and end apart: 10, of which 10 were waited for; matrix products, arithmetic and copies ran while one was open for 6% of the time, Pallas kernels for 0%

commit v1 on v0

--- a/solution.py
+++ b/solution.py
@@ -8,6 +8,30 @@
 KVH = 4
 DH = 128
 BLOCK = 256
+
+
+def figure_detail(own_rows):
+    dev_axis = "seq"
+    arr_now, local_now, known = (
+        jax.lax.axis_size(dev_axis),
+        jax.lax.axis_index(dev_axis),
+        own_rows.shape[0],
+    )
+    inter, val2 = (own_rows, 1)
+    while val2 < arr_now:
+        inter = jnp.concatenate(
+            [
+                inter,
+                jax.lax.ppermute(
+                    inter,
+                    axis_name=dev_axis,
+                    perm=[(dev_j, (dev_j - val2) % arr_now) for dev_j in range(arr_now)],
+                ),
+            ],
+            axis=0,
+        )
+        val2 = 2 * val2
+    return jnp.roll(inter, local_now * known, axis=0)
 
 
 def from_behind(value, axis, steps):
@@ -242,7 +266,7 @@
     swap = [(x * n_seq + y, y * n_seq + x) for x in range(n_heads) for y in range(n_seq)]
     stream_t = lax.ppermute(stream, ("heads", "seq"), swap)
     lin_out = lightning_local(lin_query, lin_key, lin_value, log_decay)
-    lin_all = lax.all_gather(lin_out, "seq", axis=0, tiled=True)
+    lin_all = figure_detail(lin_out)
     part = jnp.dot(lin_all, out_weight, preferred_element_type=jnp.float32).astype(jnp.bfloat16)
     own_sum = lax.psum_scatter(part, "heads", scatter_dimension=0, tiled=True)
     mixed_sum = stream_t.astype(jnp.float32) + own_sum.astype(jnp.float32)

time: 571 us -> 628 us (1.100)
  waiting for transfers between devices: 378 us -> 428 us
  local copies, waits for them, and re-layouts: 38.9 us -> 46.6 us
    ppermute x0 -> x2, waiting for transfers between devices: none -> 114 us  [figure_detail(): jax.lax.ppermute(inter, axis_name=dev_axis, perm=[(dev_j, (dev_j - val2)...]
    all_gather x1 -> x0, waiting for transfers between devices: 67.9 us -> none  [shards_fast(): lin_all = lax.all_gather(lin_out, 'seq', axis=0, tiled=True)]
    ppermute x0 -> x2, starting transfers between devices: none -> 13 us  [figure_detail(): jax.lax.ppermute(inter, axis_name=dev_axis, perm=[(dev_j, (dev_j - val2)...]
    reduce_scatter x1, starting transfers between devices: 11.4 us -> 0.42 us  [shards_fast(): own_sum = lax.psum_scatter(part, 'heads', scatter_dimension=0, tiled=True)]
    unnamed x43 -> x54, local copies, waits for them, and re-layouts: 25.2 us -> 31.1 us
  transfers between devices with their start and end apart: 10 -> 11, of which waited for: 10 -> 11; matrix products, arithmetic and copies ran while one was open for 6% -> 6% of each run, Pallas kernels for 0% -> 0%
where the time goes in v1:
time: 628 us; the launch traced here: 623 us
  waiting for transfers between devices  428 us (68%)
  matrix products  68 us (11%)
  local copies, waits for them, and re-layouts  46.6 us (7%)
  other arithmetic  28.9 us (5%)
  starting transfers between devices  21.6 us (3%)
  blocking collectives  15.5 us (2%)
  between operations  14.4 us (2%)
    ppermute x2, waiting for transfers between devices, figure_detail(): jax.lax.ppermute(inter, axis_name=dev_axis, perm=[(dev_j, (dev_j - val2)...  114 us
    ppermute x1, waiting for transfers between devices, shards_fast(): lax.ppermute(mixed_sum.astype(jnp.bfloat16), ('heads', 'seq'), swap)  101 us
    all_gather x1, waiting for transfers between devices, shards_fast(): normed_all = lax.all_gather(normed, 'heads', axis=0, tiled=True)  46.5 us
    reduce_scatter x1, waiting for transfers between devices, shards_fast(): own_sum = lax.psum_scatter(part, 'heads', scatter_dimension=0, tiled=True)  44.8 us
    reduce_scatter x1, waiting for transfers between devices, shards_fast(): reduced = lax.psum_scatter(part2, 'seq', scatter_dimension=0, tiled=True)  41.8 us
    unnamed x54, local copies, waits for them, and re-layouts  31.1 us
    ppermute x1, waiting for transfers between devices, shards_fast(): stream_t = lax.ppermute(stream, ('heads', 'seq'), swap)  29.6 us
    ppermute x3, waiting for transfers between devices, from_behind(): lax.ppermute(value, axis, [(source, source + steps) for source in range(l...  29.5 us
  transfers between devices with their start and end apart: 11, of which 11 were waited for; matrix products, arithmetic and copies ran while one was open for 6% of the time, Pallas kernels for 0%

profile of v1, /device:TPU:28, one launch (start us, length us, event | category | flops | bytes accessed | tf_op | source)
XLA Modules:
  0.0 623.1 jit_solution(10827499381382803574)
XLA Ops:
  11.2 2.2 fusion.110
  13.4 2.1 copy.237
  15.5 2.2 fusion.111
  17.7 2.0 copy.238
  19.8 2.0 copy.239
  21.8 2.0 copy.240
  23.8 1.9 convolution_add_fusion.1
  26.5 1.9 fusion.44
  29.3 3.3 maximum_bitcast_fusion
  33.2 2.2 fusion.109
  36.7 2.1 copy.242
  38.8 2.0 copy.241
  41.0 3.4 fusion.39
  44.4 4.3 fusion.43
  48.7 3.3 fusion.41
  52.0 4.5 fusion.42
  56.5 20.7 %all-gather.7.cloned.1.call-done = bf16[4,1,131080]{2,1,0:T(2,128)(2,1)} async-done(((bf16[1,1,131080]{2,1,0:T(2,128)(2,1)}), bf16[4,1,131080]{2,1,0:T(2,128)(2,1)}) %all-gather.7.cloned.1.call-update) | async-done | bytes 1048656 | tf_op jit(solution)/shard_map/all_gather | solution.py:209
  77.2 2.6 copy.280
  79.9 1.3 slice_bitcast_fusion.1
  81.3 1.5 copy.246
  83.5 2.7 multiply_reduce_fusion.2
  86.2 1.5 multiply_convert_fusion.1
  87.7 2.3 copy.188
  90.0 13.0 %collective-permute-start.1 = (bf16[512,1024]{0,1:T(8,128)(2,1)}, bf16[512,1024]{0,1:T(8,128)(2,1)S(1)}, u32[]{:S(2)}, u32[]{:S(2)}) collective-permute-start(bf16[512,1024]{0,1:T(8,128)(2,1)} %bitcast.284), channel_id=1, source_target_pairs={{0,3},{1,0},{2,1},{3,2},{4,7},{5,4},{6,5},{7,6},{8,11},{9,8},{10,9... | collective-permute-start | bytes 3145736 | tf_op jit(solution)/shard_map/ppermute | solution.py:25
  103.0 25.6 %collective-permute-done.1 = bf16[512,1024]{0,1:T(8,128)(2,1)S(1)} collective-permute-done((bf16[512,1024]{0,1:T(8,128)(2,1)}, bf16[512,1024]{0,1:T(8,128)(2,1)S(1)}, u32[]{:S(2)}, u32[]{:S(2)}) %collective-permute-start.1) | collective-permute-done | bytes 1048608 | tf_op jit(solution)/shard_map/ppermute | solution.py:25
  129.5 2.9 pad_maximum_fusion
  132.4 1.5 constant_dynamic-update-slice_fusion.5
  133.8 1.5 constant_dynamic-update-slice_fusion.4
  135.3 88.4 %collective-permute-done.2 = bf16[1024,1024]{0,1:T(8,128)(2,1)} collective-permute-done((bf16[1024,1024]{0,1:T(8,128)(2,1)}, bf16[1024,1024]{0,1:T(8,128)(2,1)}, u32[]{:S(2)}, u32[]{:S(2)}) %collective-permute-start.2) | collective-permute-done | bytes 2097184 | tf_op jit(solution)/shard_map/ppermute | solution.py:25
  223.7 1.8 constant_dynamic-update-slice_fusion.3
  225.8 1.8 constant_dynamic-update-slice_fusion
  227.6 8.7 %convolution_convert_fusion.1 = bf16[2048,1536]{1,0:T(8,128)(2,1)} fusion(bf16[1024,1536]{1,0:T(8,128)(2,1)S(1)} %copy-done, bf16[4096,1024]{0,1:T(8,128)(2,1)S(1)} %constant_dynamic-update-slice_fusion, s32[]{:T(128)S(6)} %select_n.84), kind=kOutput, calls=%fused_computation.9 | convolution fusion | flops 6445596672 | bytes 13631492 | tf_op jit(solution)/shard_map/dot_general | solution.py:270
  236.3 1.9 collective-permute-start
  238.3 5.2 all-gather.1
  243.7 29.6 %collective-permute-done = bf16[512,1536]{1,0:T(8,128)(2,1)S(1)} collective-permute-done((bf16[512,1536]{1,0:T(8,128)(2,1)}, bf16[512,1536]{1,0:T(8,128)(2,1)S(1)}, u32[]{:S(2)}, u32[]{:S(2)}) %collective-permute-start) | collective-permute-done | bytes 1572896 | tf_op jit(solution)/shard_map/ppermute | solution.py:267
  273.3 44.8 %reduce-scatter.3.cloned.1.call-done = bf16[512,1536]{1,0:T(8,128)(2,1)} async-done(((bf16[2048,1536]{1,0:T(8,128)(2,1)}), bf16[512,1536]{1,0:T(8,128)(2,1)}) %reduce-scatter.3.cloned.1.call-update) | async-done | bytes 1572880 | tf_op jit(solution)/shard_map/reduce_scatter | solution.py:271
  318.1 2.1 multiply_reduce_fusion
  320.2 10.3 %psum.7 = f32[512]{0:T(512)S(1)} all-reduce(f32[512]{0:T(512)S(1)} %multiply_reduce_fusion), channel_id=1, replica_groups=mesh['groups'=2,'heads'=4,'seq'=4] {'seq'}, use_global_device_ids=true, to_apply=%region_12.13 | all-reduce | flops 512 | bytes 4096 | tf_op jit(solution)/shard_map/psum | solution.py:274
  330.5 2.3 multiply_convert_fusion
  334.1 46.5 %all-gather.5.cloned.1.call-done = bf16[2048,1536]{1,0:T(8,128)(2,1)} async-done(((bf16[512,1536]{1,0:T(8,128)(2,1)}), bf16[2048,1536]{1,0:T(8,128)(2,1)}) %all-gather.5.cloned.1.call-update) | async-done | bytes 6291472 | tf_op jit(solution)/shard_map/all_gather | solution.py:281
  380.6 12.9 %convolution_convert_fusion = bf16[2048,1280]{1,0:T(8,128)(2,1)} fusion(bf16[2048,1536]{1,0:T(8,128)(2,1)} %all-gather.5.cloned.1.call-done, bf16[1536,256]{1,0:T(8,128)(2,1)S(1)} %dynamic-slice_bitcast_fusion, bf16[1536,1024]{1,0:T(8,128)(2,1)} %param.16), kind=kOutput, calls=%fused_computation.8 | convolution fusion | flops 8063549440 | bytes 15466496 | tf_op jit(solution)/shard_map/dot_general | solution.py:285
  393.5 1.4 copy-done.11
  394.9 2.3 collective-permute-start.3
  397.3 1.7 compare_and_fusion.3
  399.0 101.0 %collective-permute-done.3 = bf16[512,1536]{1,0:T(8,128)(2,1)S(1)} collective-permute-done((bf16[512,1536]{1,0:T(8,128)(2,1)S(1)}, bf16[512,1536]{1,0:T(8,128)(2,1)S(1)}, u32[]{:S(2)}, u32[]{:S(2)}) %collective-permute-start.3) | collective-permute-done | bytes 1572896 | tf_op jit(solution)/shard_map/ppermute | solution.py:273
  500.0 41.8 %reduce-scatter.5.cloned.1.call-done = bf16[512,1280]{1,0:T(8,128)(2,1)} async-done(((bf16[2048,1280]{1,0:T(8,128)(2,1)}), bf16[512,1280]{1,0:T(8,128)(2,1)}) %reduce-scatter.5.cloned.1.call-update) | async-done | bytes 1310736 | tf_op jit(solution)/shard_map/reduce_scatter | solution.py:286
  542.7 1.3 collective-permute-start.4
  544.0 1.3 collective-permute-start.6
  545.3 1.3 collective-permute-start.5
  546.7 3.0 fusion
  549.7 15.3 %collective-permute-done.4 = bf16[512,256]{1,0:T(8,128)(2,1)S(1)} collective-permute-done((bf16[512,256]{1,0:T(8,128)(2,1)S(1)}, bf16[512,256]{1,0:T(8,128)(2,1)S(1)}, u32[]{:S(2)}, u32[]{:S(2)}) %collective-permute-start.4) | collective-permute-done | bytes 262176 | tf_op jit(solution)/shard_map/ppermute | solution.py:40
  565.0 1.5 fusion.1
  566.5 4.6 collective-permute-done.6
  571.1 1.6 fusion.3
  572.6 9.7 %collective-permute-done.5 = bf16[512,256]{1,0:T(8,128)(2,1)S(1)} collective-permute-done((bf16[512,256]{1,0:T(8,128)(2,1)S(1)}, bf16[512,256]{1,0:T(8,128)(2,1)S(1)}, u32[]{:S(2)}, u32[]{:S(2)}) %collective-permute-start.5) | collective-permute-done | bytes 262176 | tf_op jit(solution)/shard_map/ppermute | solution.py:40
  582.3 4.8 fusion.2
  587.1 4.2 fusion.4
  591.3 6.3 %fusion.8 = (f32[8,512]{1,0:T(8,128)S(1)}, f32[8,512]{1,0:T(8,128)S(1)}) fusion(f32[512,512,8]{1,0,2:T(8,128)} %get-tuple-element.46, f32[8,512]{1,0:T(8,128)S(1)} %get-tuple-element.18, pred[512,512]{0,1:T(8,128)(4,1)S(1)} %copy-done.12, f32[8,512]{1,0:T(8,128)S(1)} %get-tuple-element.17, f32[512,512,8]{1,0,2:T(8,128)S(1)} %get-tuple-element.44, ...), kind=kLoop, calls=%fused_computation.18 | loop fusion | flops 20963328 | bytes 17367040 | tf_op jit(solution)/shard_map/reduce_sum | solution.py:248
  597.7 2.2 fusion.19
  599.9 2.2 fusion.17
  602.0 5.6 fusion.15
  607.6 3.8 fusion.32
  611.4 2.3 copy.201
  613.7 2.7 copy.287
  (97 shorter events, 12.3 us)
Async XLA Ops:
  7.2 220.4 %copy-start = (bf16[1024,1536]{1,0:T(8,128)(2,1)S(1)}, bf16[1024,1536]{1,0:T(8,128)(2,1)}, u32[]{:S(2)}) copy-start(bf16[1024,1536]{1,0:T(8,128)(2,1)} %param.14) | copy-start | bytes 9437188
  7.2 70.1 %all-gather.7.cloned.1.call-start = ((), (), s32[]{:S(2)}) async-start(), calls=%async_computation.5 | async-start | bytes 2624000 | tf_op jit(solution)/shard_map/all_gather | solution.py:209
  23.8 11.6 %copy-start.15 = (f32[512,8]{0,1:T(8,128)S(1)}, f32[512,8]{0,1:T(8,128)}, u32[]{:S(2)}) copy-start(f32[512,8]{0,1:T(8,128)} %param.12) | copy-start | bytes 49156
  25.7 0.8 copy-start.6
  32.6 285.5 %reduce-scatter.3.cloned.1.call-start = ((), (), s32[]{:S(2)}) async-start(), calls=%async_computation.2 | async-start | bytes 7864320 | tf_op jit(solution)/shard_map/reduce_scatter | solution.py:271
  81.3 1.9 copy-start.7
  81.3 1.9 copy-start.8
  81.3 2.2 copy-start.9
  90.0 38.5 %collective-permute-start.1 = (bf16[512,1024]{0,1:T(8,128)(2,1)}, bf16[512,1024]{0,1:T(8,128)(2,1)S(1)}, u32[]{:S(2)}, u32[]{:S(2)}) collective-permute-start(bf16[512,1024]{0,1:T(8,128)(2,1)} %bitcast.284), channel_id=1, source_target_pairs={{0,3},{1,0},{2,1},{3,2},{4,7},{5,4},{6,5},{7,6},{8,11},{9,8},{10,9... | collective-permute-start | bytes 3145736 | tf_op jit(solution)/shard_map/ppermute | solution.py:25
  128.5 1.0 copy-start.3
  132.4 91.3 %collective-permute-start.2 = (bf16[1024,1024]{0,1:T(8,128)(2,1)}, bf16[1024,1024]{0,1:T(8,128)(2,1)}, u32[]{:S(2)}, u32[]{:S(2)}) collective-permute-start(bf16[1024,1024]{0,1:T(8,128)(2,1)} %pad_maximum_fusion), channel_id=1, source_target_pairs={{0,2},{1,3},{2,0},{3,1},{4,6},{5,7},{6,4},{7,5},{8,10},{9,11},{10,... | collective-permute-start | bytes 6291464 | tf_op jit(solution)/shard_map/ppermute | solution.py:25
  132.4 93.1 %copy-start.2 = (bf16[512,8,128]{0,2,1:T(8,128)(2,1)S(1)}, bf16[512,8,128]{0,2,1:T(8,128)(2,1)}, u32[]{:S(2)}) copy-start(bf16[512,8,128]{0,2,1:T(8,128)(2,1)} %copy.188) | copy-start | bytes 3145732
  133.8 91.8 %copy-start.4 = (bf16[512,1024]{0,1:T(8,128)(2,1)S(1)}, bf16[512,1024]{0,1:T(8,128)(2,1)}, u32[]{:S(2)}) copy-start(bf16[512,1024]{0,1:T(8,128)(2,1)} %copy-done.3) | copy-start | bytes 3145732
  236.2 2.0 copy-start.17
  236.3 144.3 %all-gather.5.cloned.1.call-start = ((), (), s32[]{:S(2)}) async-start(), calls=%async_computation.3 | async-start | bytes 7864320 | tf_op jit(solution)/shard_map/all_gather | solution.py:281
  236.3 36.9 %collective-permute-start = (bf16[512,1536]{1,0:T(8,128)(2,1)}, bf16[512,1536]{1,0:T(8,128)(2,1)S(1)}, u32[]{:S(2)}, u32[]{:S(2)}) collective-permute-start(bf16[512,1536]{1,0:T(8,128)(2,1)} %param.13), channel_id=1, source_target_pairs={{0,0},{1,4},{2,8},{3,12},{4,1},{5,5},{6,9},{7,13},{8,2},{9,6},{10,... | collective-permute-start | bytes 4718600 | tf_op jit(solution)/shard_map/ppermute | solution.py:267
  318.1 12.4 %copy-start.5 = (bf16[512,1536]{1,0:T(8,128)(2,1)S(1)}, bf16[512,1536]{1,0:T(8,128)(2,1)}, u32[]{:S(2)}) copy-start(bf16[512,1536]{1,0:T(8,128)(2,1)} %reduce-scatter.3.cloned.1.call-done) | copy-start | bytes 4718596
  332.8 208.9 %reduce-scatter.5.cloned.1.call-start = ((), (), s32[]{:S(2)}) async-start(), calls=%async_computation.4 | async-start | bytes 6553600 | tf_op jit(solution)/shard_map/reduce_scatter | solution.py:286
  393.5 1.4 copy-start.11
  394.9 105.1 %collective-permute-start.3 = (bf16[512,1536]{1,0:T(8,128)(2,1)S(1)}, bf16[512,1536]{1,0:T(8,128)(2,1)S(1)}, u32[]{:S(2)}, u32[]{:S(2)}) collective-permute-start(bf16[512,1536]{1,0:T(8,128)(2,1)S(1)} %copy-done.11), channel_id=1, source_target_pairs={{0,0},{1,4},{2,8},{3,12},{4,1},{5,5},{6,9},{7,13},{8,2},{9,6},{10,... | collective-permute-start | bytes 4718600 | tf_op jit(solution)/shard_map/ppermute | solution.py:273
  500.0 49.7 %copy-start.10 = (bf16[512,1536]{1,0:T(8,128)(2,1)}, bf16[512,1536]{1,0:T(8,128)(2,1)S(1)}, u32[]{:S(2)}) copy-start(bf16[512,1536]{1,0:T(8,128)(2,1)S(1)} %collective-permute-done.3) | copy-start | bytes 4718596
  542.7 22.2 %collective-permute-start.4 = (bf16[512,256]{1,0:T(8,128)(2,1)S(1)}, bf16[512,256]{1,0:T(8,128)(2,1)S(1)}, u32[]{:S(2)}, u32[]{:S(2)}) collective-permute-start(bf16[512,256]{1,0:T(8,128)(2,1)S(1)} %slice.154), channel_id=1, source_target_pairs={{0,1},{1,2},{2,3},{4,5},{5,6},{6,7},{8,9},{9,10},{10,11},{12,13},{... | collective-permute-start | bytes 786440 | tf_op jit(solution)/shard_map/ppermute | solution.py:40
  544.0 27.0 %collective-permute-start.6 = (bf16[512,256]{1,0:T(8,128)(2,1)S(1)}, bf16[512,256]{1,0:T(8,128)(2,1)S(1)}, u32[]{:S(2)}, u32[]{:S(2)}) collective-permute-start(bf16[512,256]{1,0:T(8,128)(2,1)S(1)} %slice.154), channel_id=1, source_target_pairs={{0,3},{4,7},{8,11},{12,15},{16,19},{20,23},{24,27},{28,31}} | collective-permute-start | bytes 786440 | tf_op jit(solution)/shard_map/ppermute | solution.py:40
  545.3 37.0 %collective-permute-start.5 = (bf16[512,256]{1,0:T(8,128)(2,1)S(1)}, bf16[512,256]{1,0:T(8,128)(2,1)S(1)}, u32[]{:S(2)}, u32[]{:S(2)}) collective-permute-start(bf16[512,256]{1,0:T(8,128)(2,1)S(1)} %slice.154), channel_id=1, source_target_pairs={{0,2},{1,3},{4,6},{5,7},{8,10},{9,11},{12,14},{13,15},{16,18},{17,... | collective-permute-start | bytes 786440 | tf_op jit(solution)/shard_map/ppermute | solution.py:40
  546.6 18.3 %copy-start.13 = (pred[512,512]{0,1:T(8,128)(4,1)S(1)}, pred[512,512]{0,1:T(8,128)(4,1)}, u32[]{:S(2)}) copy-start(pred[512,512]{0,1:T(8,128)(4,1)} %get-tuple-element.40) | copy-start | bytes 786436
  546.7 18.3 %copy-start.16 = (bf16[512,1280]{1,0:T(8,128)(2,1)S(1)}, bf16[512,1280]{1,0:T(8,128)(2,1)}, u32[]{:S(2)}) copy-start(bf16[512,1280]{1,0:T(8,128)(2,1)} %reduce-scatter.5.cloned.1.call-done) | copy-start | bytes 3932164
  571.1 11.2 %copy-start.12 = (pred[512,512]{0,1:T(8,128)(4,1)S(1)}, pred[512,512]{0,1:T(8,128)(4,1)}, u32[]{:S(2)}) copy-start(pred[512,512]{0,1:T(8,128)(4,1)} %get-tuple-element.39) | copy-start | bytes 786436
  582.3 4.8 copy-start.14
  607.6 8.7 %copy-start.1 = (bf16[1024,1536]{1,0:T(8,128)(2,1)S(1)}, bf16[1024,1536]{1,0:T(8,128)(2,1)}, u32[]{:S(2)}) copy-start(bf16[1024,1536]{1,0:T(8,128)(2,1)} %param.14) | copy-start | bytes 9437188
Sparse Core Ops, SparseCore 0:
  32.7 44.4 all-gather.6
  236.4 81.6 reduce-scatter.2
  333.0 47.5 all-gather.4
  393.6 148.1 reduce-scatter.4
